TPU v7x, 32 devices: a whole 2x2x4 slice. The times are simulated.
32 devices in a mesh: dp: 4 (over y, x), expert: 8 (over z, core).
Axes of the slice: x: 2, y: 2, z: 4, core: 2. Of those that a mesh axis runs over, the one named last changes fastest.
Arguments:
- tokens: bfloat16 [4096, 4096], P(('dp', 'expert')), may hold values from -6 to 6
- expert_ids: int32 [4096, 2], P(('dp', 'expert')), may hold values from 0 to 7, all different within a row; in each aligned block of 128 rows (0 to 127, 128 to 255, ...) at most 64 rows name the same one
- combine: float32 [4096, 2], P(('dp', 'expert')), may hold values from 0.2 to 1
- weight_gate: bfloat16 [8, 768, 4096], P('expert'), may hold values from -0.09375 to 0.09375
- weight_up: bfloat16 [8, 768, 4096], P('expert'), may hold values from -0.09375 to 0.09375
- weight_down: bfloat16 [8, 768, 4096], P('expert'), may hold values from -0.21875 to 0.21875
- grad_out: bfloat16 [4096, 4096], P(('dp', 'expert')), may hold values from -6 to 6
Outputs:
- mixed: bfloat16 [4096, 4096], P(('dp', 'expert'))
- grad_tokens: bfloat16 [4096, 4096], P(('dp', 'expert'))
- grad_combine: float32 [4096, 2], P(('dp', 'expert'))
- grad_gate: bfloat16 [8, 768, 4096], P('expert', 'dp')
- grad_up: bfloat16 [8, 768, 4096], P('expert', 'dp')
- grad_down: bfloat16 [8, 768, 4096], P('expert', 'dp')
Inputs may be any that keep to these rules, and one draw needn't show every extreme that they name: `expert_ids`: each row names 2 different experts. In the rows of one device no expert is named more than 64 times, a bound that some block reaches.
All inputs are finite; a program needn't handle non-finite values.
Results may differ from a plain program's by a relative error of at most 0.012.
Values may be sent and summed in bfloat16 or wider, within the bound.
No kernel may reach another device: no remote copies, remote signals or barrier semaphores. Data moves between devices by JAX's collectives and lax.ppermute only.
A program may use at most 192 MiB of HBM per device.

v0:
```python
import jax
import jax.numpy as jnp
from jax import lax
from jax.sharding import PartitionSpec as P


def slot_targets(expert_ids, experts, capacity):
    tok_count, top_count = expert_ids.shape
    pair_total = tok_count * top_count
    flat_ids = expert_ids.reshape(pair_total)
    onehot = (flat_ids[:, None] == jnp.arange(experts, dtype=jnp.int32)[None, :]).astype(jnp.int32)
    earlier = jnp.cumsum(onehot, axis=0) - onehot
    position = jnp.sum(earlier * onehot, axis=1)
    return (flat_ids * capacity + position).reshape(tok_count, top_count)


def per_device(tokens, expert_ids, combine, weight_gate, weight_up, weight_down, grad_out):
    tok_count, top_count = expert_ids.shape
    model_width = tokens.shape[1]
    experts = lax.axis_size("expert")
    copies = lax.axis_size("dp")
    capacity = 2 * tok_count * top_count // experts
    slots = experts * capacity
    target = slot_targets(expert_ids, experts, capacity)
    slot_iota = jnp.arange(slots, dtype=jnp.int32)
    hit = target.T[:, :, None] == slot_iota[None, None, :]
    send_onehot = jnp.any(hit, axis=0).T.astype(jnp.bfloat16)
    weight_pair = jnp.sum(
        jnp.where(hit, combine.T[:, :, None], jnp.zeros((), jnp.float32)), axis=(0, 1)
    )
    with jax.named_scope("dispatch_rows"):
        send_rows = jnp.dot(send_onehot, tokens, preferred_element_type=jnp.float32).astype(
            jnp.bfloat16
        )
        send_go = jnp.dot(send_onehot, grad_out, preferred_element_type=jnp.float32)
        send_grads = (weight_pair[:, None] * send_go).astype(jnp.bfloat16)
    send_rows = send_rows.reshape(experts, capacity, model_width)
    send_grads = send_grads.reshape(experts, capacity, model_width)
    recv_rows = lax.all_to_all(send_rows, "expert", split_axis=0, concat_axis=0, tiled=True)
    recv_rows, send_grads = lax.optimization_barrier((recv_rows, send_grads))
    recv_grads = lax.all_to_all(send_grads, "expert", split_axis=0, concat_axis=0, tiled=True)
    in_rows = recv_rows.reshape(slots, model_width)
    out_grads = recv_grads.reshape(slots, model_width)
    w_gate = weight_gate[0]
    w_up = weight_up[0]
    w_down = weight_down[0]

    def forward(rows):
        gate_pre = jnp.dot(rows, w_gate.T, preferred_element_type=jnp.float32)
        up_pre = jnp.dot(rows, w_up.T, preferred_element_type=jnp.float32)
        sigmoid_gate = jax.nn.sigmoid(gate_pre)
        activated = (gate_pre * sigmoid_gate * up_pre).astype(jnp.bfloat16)
        expert_out = jnp.dot(activated, w_down, preferred_element_type=jnp.float32).astype(
            jnp.bfloat16
        )
        return (gate_pre, up_pre, sigmoid_gate, activated, expert_out)

    always = expert_ids[0, 0] >= 0
    gate_pre, up_pre, sigmoid_gate, activated, expert_out = lax.cond(
        always, forward, forward, in_rows
    )
    back_out = lax.all_to_all(
        expert_out.reshape(experts, capacity, model_width),
        "expert",
        split_axis=0,
        concat_axis=0,
        tiled=True,
    )
    scale = (tok_count * top_count * copies) ** (-0.5)
    grad_act = jnp.dot(out_grads, w_down.T, preferred_element_type=jnp.float32)
    grad_gate_pre = (
        grad_act * up_pre * sigmoid_gate * (1.0 + gate_pre * (1.0 - sigmoid_gate))
    ).astype(jnp.bfloat16)
    grad_up_pre = (grad_act * gate_pre * sigmoid_gate).astype(jnp.bfloat16)
    row_grads = (
        jnp.dot(grad_gate_pre, w_gate, preferred_element_type=jnp.float32)
        + jnp.dot(grad_up_pre, w_up, preferred_element_type=jnp.float32)
    ).astype(jnp.bfloat16)
    back_grads = lax.all_to_all(
        row_grads.reshape(experts, capacity, model_width),
        "expert",
        split_axis=0,
        concat_axis=0,
        tiled=True,
    )
    ff_share = w_gate.shape[0] // copies
    with jax.named_scope("weight_grads"):
        down_term = (
            scale
            * jnp.einsum("rf,rd->fd", activated, out_grads, preferred_element_type=jnp.float32)
        ).astype(jnp.bfloat16)
        rows_all = lax.all_gather(in_rows, "dp", axis=0, tiled=True)
        grads_pre = jnp.concatenate([grad_gate_pre, grad_up_pre], axis=1)
        grads_all = lax.all_gather(grads_pre, "dp", axis=0, tiled=True)
        me_dp = lax.axis_index("dp")
        ff = w_gate.shape[0]
        gate_cols = lax.dynamic_slice_in_dim(grads_all, me_dp * ff_share, ff_share, 1)
        up_cols = lax.dynamic_slice_in_dim(grads_all, ff + me_dp * ff_share, ff_share, 1)
        gate_share = (
            scale * jnp.einsum("rf,rd->fd", gate_cols, rows_all, preferred_element_type=jnp.float32)
        ).astype(jnp.bfloat16)
        up_share = (
            scale * jnp.einsum("rf,rd->fd", up_cols, rows_all, preferred_element_type=jnp.float32)
        ).astype(jnp.bfloat16)
    down_share = lax.psum_scatter(down_term, "dp", scatter_dimension=0, tiled=True)
    pick_onehot = hit.reshape(top_count * tok_count, slots).astype(jnp.bfloat16)
    with jax.named_scope("combine_rows"):
        picked_out = jnp.dot(
            pick_onehot, back_out.reshape(slots, model_width), preferred_element_type=jnp.float32
        ).reshape(top_count, tok_count, model_width)
        grad_f32 = grad_out.astype(jnp.float32)
        mixed = combine[:, 0:1] * picked_out[0]
        for k in range(1, top_count):
            mixed = mixed + combine[:, k : k + 1] * picked_out[k]
        mixed = mixed.astype(jnp.bfloat16)
        grad_combine = jnp.stack(
            [jnp.sum(grad_f32 * picked_out[k], axis=1) for k in range(top_count)], axis=1
        )
        back_grads, gate_share, up_share, mixed, grad_combine = lax.optimization_barrier(
            (back_grads, gate_share, up_share, mixed, grad_combine)
        )
        picked_grads = jnp.dot(
            pick_onehot, back_grads.reshape(slots, model_width), preferred_element_type=jnp.float32
        ).reshape(top_count, tok_count, model_width)
        grad_tokens = picked_grads[0]
        for k in range(1, top_count):
            grad_tokens = grad_tokens + picked_grads[k]
        grad_tokens = grad_tokens.astype(jnp.bfloat16)
    return (mixed, grad_tokens, grad_combine, gate_share[None], up_share[None], down_share[None])


def solution(mesh):
    in_specs = (
        P(("dp", "expert"), None),
        P(("dp", "expert"), None),
        P(("dp", "expert"), None),
        P("expert", None, None),
        P("expert", None, None),
        P("expert", None, None),
        P(("dp", "expert"), None),
    )
    out_specs = (
        P(("dp", "expert"), None),
        P(("dp", "expert"), None),
        P(("dp", "expert"), None),
        P("expert", "dp", None),
        P("expert", "dp", None),
        P("expert", "dp", None),
    )
    return jax.shard_map(
        per_device, mesh=mesh, in_specs=in_specs, out_specs=out_specs, check_vma=False
    )
```

profile of v0, /device:TPU:0, one launch (start us, length us, event | category | flops | bytes accessed | tf_op | source)
XLA Modules:
  0.0 532.3 jit_solution(12989310316587515665)
XLA Ops:
  7.2 0.0 copy-start
  7.2 0.9 copy.30
  8.1 0.1 eq.51
  8.2 0.1 eq.47
  8.4 0.6 reduce-window.6
  8.9 0.2 slice_reduce_fusion
  9.2 0.1 fusion.18
  9.3 0.1 reduce_sum.39
  9.4 0.1 copy.32
  9.5 0.7 fusion.22
  10.2 0.1 fusion.14
  10.3 0.0 copy-done
  10.3 3.3 convolution_convert_fusion
  13.6 0.0 copy-start.5
  13.6 0.0 copy-start.3
  13.6 6.5 %all-to-all-start = ((bf16[8,64,4096]{2,1,0:T(8,128)(2,1)}), bf16[8,64,4096]{2,1,0:T(8,128)(2,1)}, u32[]{:S(2)}, u32[]{:S(2)}) async-start(bf16[8,64,4096]{2,1,0:T(8,128)(2,1)} %bitcast.69), calls=%async_computation | async-start | bytes 8388608 | tf_op jit(solution)/shard_map/all_to_all | solution.py:39
  20.1 0.0 copy-done.5
  20.1 0.1 select_reduce_fusion
  20.2 0.0 copy-done.3
  20.2 3.3 multiply_convert_fusion.1
  23.5 90.7 %all-to-all-done = bf16[8,64,4096]{2,1,0:T(8,128)(2,1)} async-done(((bf16[8,64,4096]{2,1,0:T(8,128)(2,1)}), bf16[8,64,4096]{2,1,0:T(8,128)(2,1)}, u32[]{:S(2)}, u32[]{:S(2)}) %all-to-all-start) | async-done | bytes 4194336 | tf_op jit(solution)/shard_map/all_to_all | solution.py:39
  114.2 0.0 copy-start.4
  114.2 4.7 all-to-all-start.1
  118.9 0.0 all-gather.3.cloned.1.call-start
  118.9 0.0 copy-done.4
  118.9 0.5 slice.35
  120.1 23.4 %conditional.2 = (f32[512,768]{1,0:T(8,128)}, f32[512,768]{1,0:T(8,128)}, f32[512,768]{1,0:T(8,128)}, bf16[512,768]{1,0:T(8,128)(2,1)}, bf16[512,4096]{1,0:T(8,128)(2,1)}) conditional(s32[]{:T(128)} %bitcast.8, (bf16[512,4096]{1,0:T(8,128)(2,1)}, bf16[768,4096]{1,0:T(8,128)(2,1)}, bf16[768,4096]{1,0:T(8,128)(2,1)}, ...), branch_computations={%region_5.6_spmd, %region_6.7_spmd} | conditional | flops 9666035712 | bytes 83361904
  120.4 0.0 copy-start.7
  120.4 0.0 slice-start.2
  120.4 8.8 %fusion.31 = f32[512,768]{1,0:T(8,128)} fusion(bf16[512,4096]{1,0:T(8,128)(2,1)} %get-tuple-element.27, bf16[768,4096]{1,0:T(8,128)(2,1)} %get-tuple-element.28), kind=kOutput, calls=%fused_computation.59 | convolution fusion | flops 3221225472 | bytes 12058624 | tf_op jit(solution)/shard_map/cond/branch_1_fun/dot_general | solution.py:49
  129.2 0.0 copy-done.7
  129.2 0.0 slice-start.3
  129.2 8.2 %multiply_multiply_fusion.1 = (bf16[512,768]{1,0:T(8,128)(2,1)}, f32[512,768]{1,0:T(8,128)}, f32[512,768]{1,0:T(8,128)}) fusion(f32[512,768]{1,0:T(8,128)} %fusion.31, bf16[512,4096]{1,0:T(8,128)(2,1)} %get-tuple-element.27, bf16[768,4096]{1,0:T(8,128)(2,1)S(1)} %copy-done.7), kind=kOutput, calls=%fused_computation.4 | convolution fusion | flops 3223584768 | bytes 15990784 | tf_op jit(solution)/shard_map/cond/branch_1_fun/dot_general | solution.py:50
  137.4 0.0 slice-done.2
  137.4 0.0 slice-done.3
  137.4 6.1 %fusion.32 = bf16[512,4096]{1,0:T(8,128)(2,1)} fusion(bf16[512,768]{1,0:T(8,128)(2,1)} %get-tuple-element.84, bf16[768,4096]{1,0:T(8,128)(2,1)S(1)} %bitcast.83), kind=kOutput, calls=%fused_computation.60 | convolution fusion | flops 3221225472 | bytes 11272192 | tf_op jit(solution)/shard_map/cond/branch_1_fun/dot_general | solution.py:53
  143.5 69.4 %all-to-all-done.1 = bf16[8,64,4096]{2,1,0:T(8,128)(2,1)} async-done(((bf16[8,64,4096]{2,1,0:T(8,128)(2,1)}), bf16[8,64,4096]{2,1,0:T(8,128)(2,1)}, u32[]{:S(2)}, u32[]{:S(2)}) %all-to-all-start.1) | async-done | bytes 4194336 | tf_op jit(solution)/shard_map/all_to_all | solution.py:41
  212.9 9.1 %multiply_convert_fusion.2 = (bf16[512,768]{1,0:T(8,128)(2,1)S(1)}, bf16[512,768]{1,0:T(8,128)(2,1)S(1)}) fusion(f32[512,768]{1,0:T(8,128)} %get-tuple-element.52, f32[512,768]{1,0:T(8,128)} %get-tuple-element.53, f32[512,768]{1,0:T(8,128)} %get-tuple-element.51, bf16[512,4096]{1,0:T(8,128)(2,1)} %bitcast.6, bf16[1,768,4096]{2,1,0:T(8,128)(2,1)} %param.14), kind=kOutput, calls=%fused_computation.24 | convolution fusion | flops 3225157632 | bytes 16777216 | tf_op jit(solution)/shard_map/dot_general | solution.py:70
  221.9 1.3 pad_maximum_fusion
  223.2 0.0 all-gather.3.cloned.1.call-update
  223.2 0.0 all-gather.5.cloned.1.call-start
  223.3 0.7 all-gather.5.cloned.1.call-update
  224.0 4.6 all-to-all-start.3
  228.6 0.5 reduce-scatter.2.cloned.1.call-start
  229.1 9.2 %multiply_convert_fusion = bf16[768,4096]{1,0:T(8,128)(2,1)} fusion(bf16[512,4096]{1,0:T(8,128)(2,1)} %bitcast.6, bf16[512,768]{1,0:T(8,128)(2,1)} %get-tuple-element.60), kind=kOutput, calls=%fused_computation.8 | convolution fusion | flops 3227516928 | bytes 11272192 | tf_op jit(solution)/shard_map/weight_grads/rf,rd->fd/dot_general | solution.py:90
  238.3 0.0 reduce-scatter.2.cloned.1.call-update
  238.3 5.5 %fusion.25 = f32[512,4096]{1,0:T(8,128)S(1)} fusion(bf16[512,768]{1,0:T(8,128)(2,1)S(1)} %get-tuple-element.70, bf16[1,768,4096]{2,1,0:T(8,128)(2,1)} %param.12), kind=kOutput, calls=%fused_computation.53 | convolution fusion | flops 3221225472 | bytes 15466496 | tf_op jit(solution)/shard_map/dot_general | solution.py:76
  243.8 7.8 %add_convert_fusion = bf16[512,4096]{1,0:T(8,128)(2,1)} fusion(f32[512,4096]{1,0:T(8,128)S(1)} %fusion.25, bf16[512,768]{1,0:T(8,128)(2,1)S(1)} %get-tuple-element.69, bf16[1,768,4096]{2,1,0:T(8,128)(2,1)} %param.13), kind=kOutput, calls=%fused_computation.9 | convolution fusion | flops 3225419776 | bytes 19660800 | tf_op jit(solution)/shard_map/dot_general | solution.py:77
  251.7 70.9 %all-to-all-done.3 = bf16[8,64,4096]{2,1,0:T(8,128)(2,1)} async-done(((bf16[8,64,4096]{2,1,0:T(8,128)(2,1)}), bf16[8,64,4096]{2,1,0:T(8,128)(2,1)}, u32[]{:S(2)}, u32[]{:S(2)}) %all-to-all-start.3) | async-done | bytes 4194336 | tf_op jit(solution)/shard_map/all_to_all | solution.py:62
  322.6 4.7 all-to-all-start.2
  327.3 3.5 fusion.13
  330.8 2.0 fusion.6
  332.8 0.6 pad_maximum_fusion.1
  333.4 0.0 all-gather.3.cloned.1.call-done
  333.4 118.3 %all-gather.5.cloned.1.call-done = bf16[2048,4096]{1,0:T(8,128)(2,1)} async-done(((bf16[512,4096]{1,0:T(8,128)(2,1)}), bf16[2048,4096]{1,0:T(8,128)(2,1)}) %all-gather.5.cloned.1.call-update) | async-done | bytes 16777232 | tf_op jit(solution)/shard_map/weight_grads/all_gather | solution.py:92
  451.7 0.0 copy-start.2
  451.7 11.2 %fusion.5 = bf16[192,4096]{1,0:T(8,128)(2,1)} fusion(bf16[2048,4096]{1,0:T(8,128)(2,1)} %all-gather.5.cloned.1.call-done, bf16[2048,1536]{1,0:T(8,128)(2,1)} %all-gather.3.cloned.1.call-done, s32[]{:T(128)S(6)} %select_n.12), kind=kOutput, calls=%fused_computation.15 | convolution fusion | flops 3222798336 | bytes 19398660 | tf_op jit(solution)/shard_map/weight_grads/rf,rd->fd/dot_general | solution.py:103
  462.9 1.0 copy-done.2
  464.0 6.2 %fusion.4 = bf16[192,4096]{1,0:T(8,128)(2,1)} fusion(bf16[2048,4096]{1,0:T(8,128)(2,1)S(1)} %copy-done.2, bf16[2048,1536]{1,0:T(8,128)(2,1)} %all-gather.3.cloned.1.call-done, s32[]{:T(128)S(6)} %select_n.11), kind=kOutput, calls=%fused_computation.14 | convolution fusion | flops 3222798336 | bytes 19398660 | tf_op jit(solution)/shard_map/weight_grads/rf,rd->fd/dot_general | solution.py:100
  470.2 0.0 all-to-all-done.2
  470.2 3.6 fusion.12
  473.8 1.2 fusion.8
  475.0 50.6 %reduce-scatter.2.cloned.1.call-done = bf16[192,4096]{1,0:T(8,128)(2,1)} async-done(((bf16[768,4096]{1,0:T(8,128)(2,1)}), bf16[192,4096]{1,0:T(8,128)(2,1)}) %reduce-scatter.2.cloned.1.call-update) | async-done | bytes 1572880 | tf_op jit(solution)/shard_map/reduce_scatter | solution.py:105
  525.5 0.0 copy-done.1
  (6 shorter events, 0.1 us)
Async XLA Ops:
  7.2 3.2 copy-start
  13.6 6.5 %copy-start.5 = (f32[128,2]{0,1:T(2,128)S(1)}, f32[128,2]{0,1:T(2,128)}, u32[]{:S(2)}) copy-start(f32[128,2]{0,1:T(2,128)} %param.11) | copy-start | bytes 3076
  13.6 6.6 %copy-start.3 = (bf16[128,4096]{1,0:T(8,128)(2,1)S(1)}, bf16[128,4096]{1,0:T(8,128)(2,1)}, u32[]{:S(2)}) copy-start(bf16[128,4096]{1,0:T(8,128)(2,1)} %param.15) | copy-start | bytes 3145732
  13.6 100.6 %all-to-all-start = ((bf16[8,64,4096]{2,1,0:T(8,128)(2,1)}), bf16[8,64,4096]{2,1,0:T(8,128)(2,1)}, u32[]{:S(2)}, u32[]{:S(2)}) async-start(bf16[8,64,4096]{2,1,0:T(8,128)(2,1)} %bitcast.69), calls=%async_computation | async-start | bytes 8388608 | tf_op jit(solution)/shard_map/all_to_all | solution.py:39
  114.2 4.7 copy-start.4
  114.2 98.7 %all-to-all-start.1 = ((bf16[8,64,4096]{2,1,0:T(8,128)(2,1)}), bf16[8,64,4096]{2,1,0:T(8,128)(2,1)}, u32[]{:S(2)}, u32[]{:S(2)}) async-start(bf16[8,64,4096]{2,1,0:T(8,128)(2,1)} %bitcast.68), calls=%async_computation.1 | async-start | bytes 8388608 | tf_op jit(solution)/shard_map/all_to_all | solution.py:41
  118.9 214.5 %all-gather.3.cloned.1.call-start = ((), (), s32[]{:S(2)}) async-start(), calls=%async_computation.5 | async-start | bytes 7864320 | tf_op jit(solution)/shard_map/weight_grads/all_gather | solution.py:94
  120.4 8.8 %copy-start.7 = (bf16[768,4096]{1,0:T(8,128)(2,1)S(1)}, bf16[768,4096]{1,0:T(8,128)(2,1)}, u32[]{:S(2)}) copy-start(bf16[768,4096]{1,0:T(8,128)(2,1)} %get-tuple-element.29) | copy-start | bytes 18874372 | tf_op jit(solution)/shard_map/conditional
  120.4 17.0 %slice-start.2 = ((s8[6291456]{0:T(1024)(128)(4,1)}), s8[4194304]{0:T(1024)(128)(4,1)S(1)}, s32[]{:S(2)}) async-start(s8[6291456]{0:T(1024)(128)(4,1)} %bitcast.82), calls=%async_computation.10 | async-start | bytes 8388608 | tf_op jit(solution)/shard_map/conditional
  129.2 8.2 %slice-start.3 = ((s8[6291456]{0:T(1024)(128)(4,1)}), s8[2097152]{0:T(1024)(128)(4,1)S(1)}, s32[]{:S(2)}) async-start(s8[6291456]{0:T(1024)(128)(4,1)} %bitcast.82), calls=%async_computation.11 | async-start | bytes 4194304 | tf_op jit(solution)/shard_map/conditional
  223.2 228.5 %all-gather.5.cloned.1.call-start = ((), (), s32[]{:S(2)}) async-start(), calls=%async_computation.6 | async-start | bytes 20971520 | tf_op jit(solution)/shard_map/weight_grads/all_gather | solution.py:92
  224.0 98.6 %all-to-all-start.3 = ((bf16[8,64,4096]{2,1,0:T(8,128)(2,1)}), bf16[8,64,4096]{2,1,0:T(8,128)(2,1)}, u32[]{:S(2)}, u32[]{:S(2)}) async-start(bf16[8,64,4096]{2,1,0:T(8,128)(2,1)} %bitcast.15), calls=%async_computation.3 | async-start | bytes 8388608 | tf_op jit(solution)/shard_map/all_to_all | solution.py:62
  228.6 297.0 %reduce-scatter.2.cloned.1.call-start = ((), (), s32[]{:S(2)}) async-start(), calls=%async_computation.7 | async-start | bytes 7864320 | tf_op jit(solution)/shard_map/reduce_scatter | solution.py:105
  322.6 147.6 %all-to-all-start.2 = ((bf16[8,64,4096]{2,1,0:T(8,128)(2,1)}), bf16[8,64,4096]{2,1,0:T(8,128)(2,1)}, u32[]{:S(2)}, u32[]{:S(2)}) async-start(bf16[8,64,4096]{2,1,0:T(8,128)(2,1)} %bitcast.72), calls=%async_computation.2 | async-start | bytes 8388608 | tf_op jit(solution)/shard_map/all_to_all | solution.py:79
  451.7 12.2 %copy-start.2 = (bf16[2048,4096]{1,0:T(8,128)(2,1)S(1)}, bf16[2048,4096]{1,0:T(8,128)(2,1)}, u32[]{:S(2)}) copy-start(bf16[2048,4096]{1,0:T(8,128)(2,1)} %all-gather.5.cloned.1.call-done) | copy-start | bytes 50331652
  470.2 55.4 %copy-start.1 = (bf16[128,4096]{1,0:T(8,128)(2,1)S(1)}, bf16[128,4096]{1,0:T(8,128)(2,1)}, u32[]{:S(2)}) copy-start(bf16[128,4096]{1,0:T(8,128)(2,1)} %param.9) | copy-start | bytes 3145732
Sparse Core Ops, SparseCore 0:
  223.3 69.0 all-gather.2
  294.3 157.4 all-gather.4
  455.3 70.2 reduce-scatter.1
where the time goes:
time: 540 us; the launch traced here: 532 us
  waiting for transfers between devices  401 us (74%)
  matrix products  85.7 us (16%)
  starting transfers between devices  21 us (4%)
  between operations  14.7 us (3%)
  other arithmetic  6.73 us (1%)
    all_gather x1, waiting for transfers between devices, per_device(): rows_all = lax.all_gather(in_rows, 'dp', axis=0, tiled=True)  118 us
    all_to_all x1, waiting for transfers between devices, per_device(): lax.all_to_all(send_rows, 'expert', split_axis=0, concat_axis=0, tiled=True)  90.7 us
    all_to_all x1, waiting for transfers between devices, per_device(): lax.all_to_all(expert_out.reshape(experts, capacity, model_width), 'exper...  70.9 us
    all_to_all x1, waiting for transfers between devices, per_device(): lax.all_to_all(send_grads, 'expert', split_axis=0, concat_axis=0, tiled=T...  69.4 us
    reduce_scatter x1, waiting for transfers between devices, per_device(): lax.psum_scatter(down_term, 'dp', scatter_dimension=0, tiled=True)  50.6 us
    dot_general x1, matrix products, per_device(): jnp.einsum('rf,rd->fd', up_cols, rows_all, preferred_element_type=jnp.flo...  11.2 us
  transfers between devices with their start and end apart: 7, of which 5 were waited for; matrix products, arithmetic and copies ran while one was open for 15% of the time, Pallas kernels for 0%

commit v1 on v0

--- a/solution.py
+++ b/solution.py
@@ -89,7 +89,27 @@
             scale
             * jnp.einsum("rf,rd->fd", activated, out_grads, preferred_element_type=jnp.float32)
         ).astype(jnp.bfloat16)
-        rows_all = lax.all_gather(in_rows, "dp", axis=0, tiled=True)
+        part_now = lax.psum(1, axis_name="dp")
+        o_now = lax.axis_index("dp")
+        shaped, near, response = (part_now, o_now, in_rows.shape[0])
+        heap = [(i0, (i0 + 1) % shaped) for i0 in range(shaped)]
+        sides = [(i0, (i0 - 1) % shaped) for i0 in range(shaped)]
+        rows_all = jnp.zeros(
+            (*in_rows.shape[:0], shaped * response, *in_rows.shape[1:]), in_rows.dtype
+        )
+        rows_all = lax.dynamic_update_slice_in_dim(rows_all, in_rows, near * response, axis=0)
+        w2 = z_new = in_rows
+        built = shaped // 2
+        for hop_no in range(1, built + 1):
+            w2 = lax.ppermute(w2, "dp", heap)
+            rows_all = lax.dynamic_update_slice_in_dim(
+                rows_all, w2, (near - hop_no) % shaped * response, axis=0
+            )
+            if hop_no < shaped - built:
+                z_new = lax.ppermute(z_new, "dp", perm=sides)
+                rows_all = lax.dynamic_update_slice_in_dim(
+                    rows_all, z_new, (near + hop_no) % shaped * response, axis=0
+                )
         grads_pre = jnp.concatenate([grad_gate_pre, grad_up_pre], axis=1)
         grads_all = lax.all_gather(grads_pre, "dp", axis=0, tiled=True)
         me_dp = lax.axis_index("dp")

time: 540 us -> 652 us (1.21)
  waiting for transfers between devices: 401 us -> 469 us
  local copies, waits for them, and re-layouts: 3.18 us -> 26.8 us
  loops' own time: 0.29 us -> 11.8 us
    ppermute x0 -> x3, waiting for transfers between devices: none -> 253 us  [the longest x2 155 us: per_device(): w2 = lax.ppermute(w2, 'dp', heap)]
    all_gather x1 -> x0, waiting for transfers between devices: 118 us -> none  [per_device(): rows_all = lax.all_gather(in_rows, 'dp', axis=0, tiled=True)]
    reduce_scatter x1, waiting for transfers between devices: 50.6 us -> 0.01 us  [per_device(): lax.psum_scatter(down_term, 'dp', scatter_dimension=0, tiled=True)]
    dynamic_update_slice x0 -> x4, local copies, waits for them, and re-layouts: none -> 18.7 us  [the longest x2 9.26 us: per_device(): lax.dynamic_update_slice_in_dim(rows_all, w2, (near - hop_no) % shaped *...]
    all_to_all x1, waiting for transfers between devices: 69.4 us -> 57.7 us  [per_device(): lax.all_to_all(send_grads, 'expert', split_axis=0, concat_axis=0, tiled=T...]
    unnamed x1, loops' own time: 0.29 us -> 11.8 us
  transfers between devices with their start and end apart: 7 -> 9, of which waited for: 5 -> 6; matrix products, arithmetic and copies ran while one was open for 15% -> 17% of each run, Pallas kernels for 0% -> 0%
where the time goes in v1:
time: 652 us; the launch traced here: 644 us
  waiting for transfers between devices  469 us (72%)
  matrix products  90.5 us (14%)
  local copies, waits for them, and re-layouts  26.8 us (4%)
  starting transfers between devices  23.3 us (4%)
  between operations  15.2 us (2%)
  loops' own time  11.8 us (2%)
  other arithmetic  6.73 us (1%)
    ppermute x2, waiting for transfers between devices, per_device(): w2 = lax.ppermute(w2, 'dp', heap)  155 us
    ppermute x1, waiting for transfers between devices, per_device(): z_new = lax.ppermute(z_new, 'dp', perm=sides)  97.8 us
    all_to_all x1, waiting for transfers between devices, per_device(): lax.all_to_all(send_rows, 'expert', split_axis=0, concat_axis=0, tiled=True)  90.7 us
    all_to_all x1, waiting for transfers between devices, per_device(): lax.all_to_all(expert_out.reshape(experts, capacity, model_width), 'exper...  68.3 us
    all_to_all x1, waiting for transfers between devices, per_device(): lax.all_to_all(send_grads, 'expert', split_axis=0, concat_axis=0, tiled=T...  57.7 us
  transfers between devices with their start and end apart: 9, of which 6 were waited for; matrix products, arithmetic and copies ran while one was open for 17% of the time, Pallas kernels for 0%

profile of v1, /device:TPU:0, one launch (start us, length us, event | category | flops | bytes accessed | tf_op | source)
XLA Modules:
  0.0 643.8 jit_solution(10339565204439641524)
XLA Ops:
  7.2 0.0 copy-start
  7.2 0.9 copy.30
  8.1 0.1 eq.55
  8.2 0.1 eq.51
  8.4 0.6 reduce-window.6
  8.9 0.2 slice_reduce_fusion
  9.2 0.1 fusion.18
  9.3 0.1 reduce_sum.39
  9.4 0.1 copy.32
  9.5 0.7 fusion.22
  10.2 0.1 fusion.14
  10.3 0.0 copy-done
  10.3 3.3 convolution_convert_fusion
  13.6 6.5 %all-to-all-start = ((bf16[8,64,4096]{2,1,0:T(8,128)(2,1)}), bf16[8,64,4096]{2,1,0:T(8,128)(2,1)}, u32[]{:S(2)}, u32[]{:S(2)}) async-start(bf16[8,64,4096]{2,1,0:T(8,128)(2,1)} %bitcast.69), calls=%async_computation | async-start | bytes 8388608 | tf_op jit(solution)/shard_map/all_to_all | solution.py:39
  20.1 0.0 copy-done.4
  20.1 0.1 select_reduce_fusion
  20.2 0.0 copy-done.2
  20.2 3.2 multiply_convert_fusion.1
  23.5 90.7 %all-to-all-done = bf16[8,64,4096]{2,1,0:T(8,128)(2,1)} async-done(((bf16[8,64,4096]{2,1,0:T(8,128)(2,1)}), bf16[8,64,4096]{2,1,0:T(8,128)(2,1)}, u32[]{:S(2)}, u32[]{:S(2)}) %all-to-all-start) | async-done | bytes 4194336 | tf_op jit(solution)/shard_map/all_to_all | solution.py:39
  114.2 4.7 all-to-all-start.1
  118.9 0.0 all-gather.2.cloned.1.call-start
  118.9 0.0 copy-done.3
  118.9 0.5 slice.35
  120.1 35.1 %conditional.2 = (f32[512,768]{1,0:T(8,128)}, f32[512,768]{1,0:T(8,128)}, f32[512,768]{1,0:T(8,128)}, bf16[512,768]{1,0:T(8,128)(2,1)}, bf16[512,4096]{1,0:T(8,128)(2,1)}) conditional(s32[]{:T(128)} %bitcast.8, (bf16[512,4096]{1,0:T(8,128)(2,1)}, bf16[768,4096]{1,0:T(8,128)(2,1)}, bf16[768,4096]{1,0:T(8,128)(2,1)}, ...), branch_computations={%region_5.6_spmd, %region_6.7_spmd} | conditional | flops 9666035712 | bytes 83361904
  131.9 0.0 copy-start.6
  131.9 0.0 slice-start.2
  131.9 8.8 %fusion.31 = f32[512,768]{1,0:T(8,128)} fusion(bf16[512,4096]{1,0:T(8,128)(2,1)} %get-tuple-element.27, bf16[768,4096]{1,0:T(8,128)(2,1)} %get-tuple-element.28), kind=kOutput, calls=%fused_computation.63 | convolution fusion | flops 3221225472 | bytes 12058624 | tf_op jit(solution)/shard_map/cond/branch_1_fun/dot_general | solution.py:49
  140.7 0.0 copy-done.6
  140.7 8.2 %multiply_multiply_fusion.1 = (bf16[512,768]{1,0:T(8,128)(2,1)}, f32[512,768]{1,0:T(8,128)}, f32[512,768]{1,0:T(8,128)}) fusion(f32[512,768]{1,0:T(8,128)} %fusion.31, bf16[512,4096]{1,0:T(8,128)(2,1)} %get-tuple-element.27, bf16[768,4096]{1,0:T(8,128)(2,1)S(1)} %copy-done.6), kind=kOutput, calls=%fused_computation.4 | convolution fusion | flops 3223584768 | bytes 15990784 | tf_op jit(solution)/shard_map/cond/branch_1_fun/dot_general | solution.py:50
  148.9 0.0 slice-done.2
  148.9 0.0 slice-done.3
  148.9 6.2 fusion.32
  155.2 57.7 %all-to-all-done.1 = bf16[8,64,4096]{2,1,0:T(8,128)(2,1)} async-done(((bf16[8,64,4096]{2,1,0:T(8,128)(2,1)}), bf16[8,64,4096]{2,1,0:T(8,128)(2,1)}, u32[]{:S(2)}, u32[]{:S(2)}) %all-to-all-start.1) | async-done | bytes 4194336 | tf_op jit(solution)/shard_map/all_to_all | solution.py:41
  212.9 8.9 %multiply_convert_fusion.2 = (bf16[512,768]{1,0:T(8,128)(2,1)S(1)}, bf16[512,768]{1,0:T(8,128)(2,1)S(1)}) fusion(f32[512,768]{1,0:T(8,128)} %get-tuple-element.52, f32[512,768]{1,0:T(8,128)} %get-tuple-element.53, f32[512,768]{1,0:T(8,128)} %get-tuple-element.51, bf16[512,4096]{1,0:T(8,128)(2,1)} %bitcast.6, bf16[1,768,4096]{2,1,0:T(8,128)(2,1)} %param.14), kind=kOutput, calls=%fused_computation.24 | convolution fusion | flops 3225157632 | bytes 16777216 | tf_op jit(solution)/shard_map/dot_general | solution.py:70
  221.8 1.3 pad_maximum_fusion
  223.1 0.0 all-gather.2.cloned.1.call-update
  223.1 4.6 all-to-all-start.3
  227.7 0.0 reduce-scatter.2.cloned.1.call-start
  227.7 9.3 %multiply_convert_fusion = bf16[768,4096]{1,0:T(8,128)(2,1)} fusion(bf16[512,4096]{1,0:T(8,128)(2,1)} %bitcast.6, bf16[512,768]{1,0:T(8,128)(2,1)} %get-tuple-element.60), kind=kOutput, calls=%fused_computation.8 | convolution fusion | flops 3227516928 | bytes 11272192 | tf_op jit(solution)/shard_map/weight_grads/rf,rd->fd/dot_general | solution.py:90
  237.0 0.0 reduce-scatter.2.cloned.1.call-update
  237.1 1.4 collective-permute-start
  238.5 1.5 collective-permute-start.1
  240.0 5.5 fusion.25
  245.6 7.8 %add_convert_fusion = bf16[512,4096]{1,0:T(8,128)(2,1)} fusion(f32[512,4096]{1,0:T(8,128)S(1)} %fusion.25, bf16[512,768]{1,0:T(8,128)(2,1)S(1)} %get-tuple-element.69, bf16[1,768,4096]{2,1,0:T(8,128)(2,1)} %param.13), kind=kOutput, calls=%fused_computation.9 | convolution fusion | flops 3225419776 | bytes 19660800 | tf_op jit(solution)/shard_map/dot_general | solution.py:77
  253.4 68.3 %all-to-all-done.3 = bf16[8,64,4096]{2,1,0:T(8,128)(2,1)} async-done(((bf16[8,64,4096]{2,1,0:T(8,128)(2,1)}), bf16[8,64,4096]{2,1,0:T(8,128)(2,1)}, u32[]{:S(2)}, u32[]{:S(2)}) %all-to-all-start.3) | async-done | bytes 4194336 | tf_op jit(solution)/shard_map/all_to_all | solution.py:62
  321.7 4.5 all-to-all-start.2
  326.2 75.0 %collective-permute-done = bf16[512,4096]{1,0:T(8,128)(2,1)} collective-permute-done((bf16[512,4096]{1,0:T(8,128)(2,1)}, bf16[512,4096]{1,0:T(8,128)(2,1)}, u32[]{:S(2)}, u32[]{:S(2)}) %collective-permute-start) | collective-permute-done | bytes 4194336 | tf_op jit(solution)/shard_map/weight_grads/ppermute | solution.py:104
  401.2 0.0 collective-permute-start.2
  401.2 6.0 broadcast_in_dim.31
  407.2 4.8 constant_dynamic-update-slice_fusion.3
  412.0 4.6 constant_dynamic-update-slice_fusion.2
  416.6 97.8 %collective-permute-done.1 = bf16[512,4096]{1,0:T(8,128)(2,1)} collective-permute-done((bf16[512,4096]{1,0:T(8,128)(2,1)}, bf16[512,4096]{1,0:T(8,128)(2,1)}, u32[]{:S(2)}, u32[]{:S(2)}) %collective-permute-start.1) | collective-permute-done | bytes 4194336 | tf_op jit(solution)/shard_map/weight_grads/ppermute | solution.py:109
  514.4 4.7 constant_dynamic-update-slice_fusion.1
  519.1 3.5 fusion.13
  522.6 2.0 fusion.6
  524.6 0.6 pad_maximum_fusion.1
  525.2 79.9 %collective-permute-done.2 = bf16[512,4096]{1,0:T(8,128)(2,1)} collective-permute-done((bf16[512,4096]{1,0:T(8,128)(2,1)}, bf16[512,4096]{1,0:T(8,128)(2,1)}, u32[]{:S(2)}, u32[]{:S(2)}) %collective-permute-start.2) | collective-permute-done | bytes 4194336 | tf_op jit(solution)/shard_map/weight_grads/ppermute | solution.py:104
  605.0 4.7 constant_dynamic-update-slice_fusion
  609.7 11.1 %fusion.5 = bf16[192,4096]{1,0:T(8,128)(2,1)} fusion(bf16[2048,4096]{1,0:T(8,128)(2,1)} %constant_dynamic-update-slice_fusion, bf16[2048,1536]{1,0:T(8,128)(2,1)} %all-gather.2.cloned.1.call-done, s32[]{:T(128)S(6)} %select_n.46), kind=kOutput, calls=%fused_computation.15 | convolution fusion | flops 3222798336 | bytes 19398660 | tf_op jit(solution)/shard_map/weight_grads/rf,rd->fd/dot_general | solution.py:123
  620.7 11.1 %fusion.4 = bf16[192,4096]{1,0:T(8,128)(2,1)} fusion(bf16[2048,4096]{1,0:T(8,128)(2,1)} %constant_dynamic-update-slice_fusion, bf16[2048,1536]{1,0:T(8,128)(2,1)} %all-gather.2.cloned.1.call-done, s32[]{:T(128)S(6)} %select_n.38), kind=kOutput, calls=%fused_computation.14 | convolution fusion | flops 3222798336 | bytes 19398660 | tf_op jit(solution)/shard_map/weight_grads/rf,rd->fd/dot_general | solution.py:120
  631.8 0.0 all-to-all-done.2
  631.8 3.6 fusion.12
  635.4 1.2 fusion.8
  636.6 0.0 copy-done.1
  (12 shorter events, 0.1 us)
Async XLA Ops:
  7.2 3.2 copy-start
  13.6 6.5 %copy-start.4 = (f32[128,2]{0,1:T(2,128)S(1)}, f32[128,2]{0,1:T(2,128)}, u32[]{:S(2)}) copy-start(f32[128,2]{0,1:T(2,128)} %param.11) | copy-start | bytes 3076
  13.6 6.6 %copy-start.2 = (bf16[128,4096]{1,0:T(8,128)(2,1)S(1)}, bf16[128,4096]{1,0:T(8,128)(2,1)}, u32[]{:S(2)}) copy-start(bf16[128,4096]{1,0:T(8,128)(2,1)} %param.15) | copy-start | bytes 3145732
  13.6 100.6 %all-to-all-start = ((bf16[8,64,4096]{2,1,0:T(8,128)(2,1)}), bf16[8,64,4096]{2,1,0:T(8,128)(2,1)}, u32[]{:S(2)}, u32[]{:S(2)}) async-start(bf16[8,64,4096]{2,1,0:T(8,128)(2,1)} %bitcast.69), calls=%async_computation | async-start | bytes 8388608 | tf_op jit(solution)/shard_map/all_to_all | solution.py:39
  114.2 4.7 copy-start.3
  114.2 98.7 %all-to-all-start.1 = ((bf16[8,64,4096]{2,1,0:T(8,128)(2,1)}), bf16[8,64,4096]{2,1,0:T(8,128)(2,1)}, u32[]{:S(2)}, u32[]{:S(2)}) async-start(bf16[8,64,4096]{2,1,0:T(8,128)(2,1)} %bitcast.68), calls=%async_computation.1 | async-start | bytes 8388608 | tf_op jit(solution)/shard_map/all_to_all | solution.py:41
  118.9 490.8 %all-gather.2.cloned.1.call-start = ((), (), s32[]{:S(2)}) async-start(), calls=%async_computation.5 | async-start | bytes 7864320 | tf_op jit(solution)/shard_map/weight_grads/all_gather | solution.py:114
  131.9 8.8 %copy-start.6 = (bf16[768,4096]{1,0:T(8,128)(2,1)S(1)}, bf16[768,4096]{1,0:T(8,128)(2,1)}, u32[]{:S(2)}) copy-start(bf16[768,4096]{1,0:T(8,128)(2,1)} %get-tuple-element.29) | copy-start | bytes 18874372 | tf_op jit(solution)/shard_map/conditional
  131.9 17.0 %slice-start.2 = ((s8[6291456]{0:T(1024)(128)(4,1)}), s8[4194304]{0:T(1024)(128)(4,1)S(1)}, s32[]{:S(2)}) async-start(s8[6291456]{0:T(1024)(128)(4,1)} %bitcast.82), calls=%async_computation.9 | async-start | bytes 8388608 | tf_op jit(solution)/shard_map/conditional
  140.7 8.2 %slice-start.3 = ((s8[6291456]{0:T(1024)(128)(4,1)}), s8[2097152]{0:T(1024)(128)(4,1)S(1)}, s32[]{:S(2)}) async-start(s8[6291456]{0:T(1024)(128)(4,1)} %bitcast.82), calls=%async_computation.10 | async-start | bytes 4194304 | tf_op jit(solution)/shard_map/conditional
  223.1 98.6 %all-to-all-start.3 = ((bf16[8,64,4096]{2,1,0:T(8,128)(2,1)}), bf16[8,64,4096]{2,1,0:T(8,128)(2,1)}, u32[]{:S(2)}, u32[]{:S(2)}) async-start(bf16[8,64,4096]{2,1,0:T(8,128)(2,1)} %bitcast.15), calls=%async_computation.3 | async-start | bytes 8388608 | tf_op jit(solution)/shard_map/all_to_all | solution.py:62
  227.7 408.9 %reduce-scatter.2.cloned.1.call-start = ((), (), s32[]{:S(2)}) async-start(), calls=%async_computation.6 | async-start | bytes 7864320 | tf_op jit(solution)/shard_map/reduce_scatter | solution.py:125
  237.1 164.1 %collective-permute-start = (bf16[512,4096]{1,0:T(8,128)(2,1)}, bf16[512,4096]{1,0:T(8,128)(2,1)}, u32[]{:S(2)}, u32[]{:S(2)}) collective-permute-start(bf16[512,4096]{1,0:T(8,128)(2,1)} %bitcast.9), channel_id=1, source_target_pairs={{0,8},{8,16},{16,24},{24,0},{1,9},{9,17},{17,25},{25,1},{2,10},{10... | collective-permute-start | bytes 12582920 | tf_op jit(solution)/shard_map/weight_grads/ppermute | solution.py:104
  238.5 275.9 %collective-permute-start.1 = (bf16[512,4096]{1,0:T(8,128)(2,1)}, bf16[512,4096]{1,0:T(8,128)(2,1)}, u32[]{:S(2)}, u32[]{:S(2)}) collective-permute-start(bf16[512,4096]{1,0:T(8,128)(2,1)} %bitcast.9), channel_id=1, source_target_pairs={{0,24},{8,0},{16,8},{24,16},{1,25},{9,1},{17,9},{25,17},{2,26},{10... | collective-permute-start | bytes 12582920 | tf_op jit(solution)/shard_map/weight_grads/ppermute | solution.py:109
  321.7 310.1 %all-to-all-start.2 = ((bf16[8,64,4096]{2,1,0:T(8,128)(2,1)}), bf16[8,64,4096]{2,1,0:T(8,128)(2,1)}, u32[]{:S(2)}, u32[]{:S(2)}) async-start(bf16[8,64,4096]{2,1,0:T(8,128)(2,1)} %bitcast.72), calls=%async_computation.2 | async-start | bytes 8388608 | tf_op jit(solution)/shard_map/all_to_all | solution.py:79
  401.2 203.8 %collective-permute-start.2 = (bf16[512,4096]{1,0:T(8,128)(2,1)}, bf16[512,4096]{1,0:T(8,128)(2,1)}, u32[]{:S(2)}, u32[]{:S(2)}) collective-permute-start(bf16[512,4096]{1,0:T(8,128)(2,1)} %collective-permute-done), channel_id=1, source_target_pairs={{0,8},{8,16},{16,24},{24,0},{1,9},{9,17},{17,25},{25,1},{2,10},{10... | collective-permute-start | bytes 12582920 | tf_op jit(solution)/shard_map/weight_grads/ppermute | solution.py:104
  631.8 4.8 copy-start.1
Sparse Core Ops, SparseCore 0:
  223.2 112.9 all-gather.1
  339.8 119.7 reduce-scatter.1
